TPU v7x, 256 devices: a whole 4x4x8 slice. The times are simulated.
256 devices in a mesh: ctx: 16 (over z_lo, x), ch: 16 (over y, z_hi, core).
Axes of the slice: x: 4, y: 4, z: 8 (z_hi: 2, z_lo: 4; z = z_hi * 4 + z_lo), core: 2. Of those that a mesh axis runs over, the one named last changes fastest.
Arguments:
- tokens: bfloat16 [4096, 8192], P('ctx', 'ch'), may hold values from -6 to 6
- in_weight: bfloat16 [8192, 3, 8192], P('ctx', None, 'ch'), may hold values from -0.0625 to 0.0625
- short_filter: bfloat16 [3, 3, 8192], P(None, None, 'ch'), may hold values from -3 to 3
- decay_rate: float32 [8192, 16], P('ch'), may hold values from 1.2207031e-05 to 0.0333333333
- residue: float32 [8192, 16], P('ch'), may hold values from -0.12 to 0.12
- skip_gain: float32 [8192], P('ch'), may hold values from -4 to 4
Outputs:
- filtered: bfloat16 [4096, 8192], P('ctx', 'ch')
All inputs are finite; a program needn't handle non-finite values.
Results may differ from a plain program's by a relative error of at most 0.007.
Values may be sent and summed in bfloat16 or wider, within the bound.
No kernel may reach another device: no remote copies, remote signals or barrier semaphores. Data moves between devices by JAX's collectives and lax.ppermute only.
A program may use at most 128 MiB of HBM per device.

v0:
```python
import jax
import jax.numpy as jnp
import numpy as np
from jax import lax
from jax.sharding import Mesh, PartitionSpec as P

exact_mode = lax.Precision.HIGHEST
SEQ = ("zl", "x")


def from_behind(block, axis, distance):
    devices = range(lax.axis_size(axis))
    route = [(i - distance, i) for i in devices if i - distance in devices]
    return lax.ppermute(block, axis, route)


def ring_sends(pieces, axis, size):
    position = lax.axis_index(axis)
    received = []
    for k in range(1, size):
        route = [(i, (i + k) % size) for i in range(size)]
        received.append(lax.ppermute(pieces(k, position), axis, route))
    return received


def local(tokens, in_weight, short_filter, decay_rate, residue, skip_gain):
    tok_rows = tokens.shape[0]
    width_local = in_weight.shape[2]
    mode_count = decay_rate.shape[1]
    feat_block = in_weight.shape[0]
    across, down = (lax.axis_size("x"), lax.axis_size("zl"))
    me_x, me_z = (lax.axis_index("x"), lax.axis_index("zl"))
    flat_own = in_weight.reshape(feat_block, 3 * width_local)
    weights = [flat_own] + ring_sends(lambda k, p: flat_own, "x", across)
    gathered = lax.all_gather(tokens, "ch", axis=1, tiled=True)
    chunk = gathered.shape[1] // down

    def chunk_for(k, p):
        return lax.dynamic_slice_in_dim(gathered, (p + k) % down * chunk, chunk, axis=1)

    rows = [chunk_for(0, me_z)] + ring_sends(chunk_for, "zl", down)
    column = jnp.concatenate(rows, axis=0)
    partial = jnp.zeros((column.shape[0], 3 * width_local), jnp.float32)
    for k in range(across):
        source = (me_x - k) % across
        taken = lax.dynamic_slice_in_dim(column, source * feat_block, feat_block, axis=1)
        partial = partial + jnp.dot(taken, weights[k], preferred_element_type=jnp.float32)
    pieces = partial.reshape(down, tok_rows, 3 * width_local)
    projected = pieces[0]
    for k in range(1, down):
        route = [(i, (i - k) % down) for i in range(down)]
        back = lax.ppermute(pieces[k].astype(jnp.bfloat16), "zl", route)
        projected = projected + back.astype(jnp.float32)
    streams = projected.astype(jnp.bfloat16).reshape(tok_rows, 3, width_local)
    tap_count = short_filter.shape[0]
    last_rows = streams[tok_rows - (tap_count - 1) :]
    before = from_behind(last_rows, SEQ, 1)
    padded = jnp.concatenate([before, streams], axis=0).astype(jnp.float32)
    filter_taps = short_filter.astype(jnp.float32)
    featured = jnp.zeros((tok_rows, 3, width_local), jnp.float32)
    for shift_back in range(tap_count):
        begin = tap_count - 1 - shift_back
        featured = featured + filter_taps[shift_back][None] * padded[begin : begin + tok_rows]
    query_gate = featured[:, 0]
    gated_rows = (featured[:, 1] * featured[:, 2]).astype(jnp.bfloat16)
    gated_wide = gated_rows.astype(jnp.float32)
    position = jnp.arange(tok_rows, dtype=jnp.float32)
    powers = jnp.exp(-decay_rate[None, :, :] * (tok_rows - 1.0 - position)[:, None, None])
    local_state = jnp.einsum("jc,jcr->cr", gated_wide, powers, precision=exact_mode)
    along = [local_state] + ring_sends(lambda k, p: local_state, "x", across)
    row = jnp.stack(along)
    states = jnp.stack([row] + ring_sends(lambda k, p: row, "zl", down))
    step_z = jnp.arange(down)[:, None]
    step_x = jnp.arange(across)[None, :]
    source = (me_z - step_z) % down * across + (me_x - step_x) % across
    lag = (me_z * across + me_x - 1 - source).astype(jnp.float32)
    decay_b = decay_rate[None, None]
    weight = jnp.exp(-decay_b * (float(tok_rows) * jnp.maximum(lag, 0.0))[:, :, None, None])
    weight = jnp.where((lag >= 0)[:, :, None, None], weight, 0.0)
    incoming = jnp.sum(weight * states, axis=(0, 1))
    growth = jnp.exp(decay_rate[None, :, :] * position[:, None, None])
    scaled = (gated_wide[:, :, None] * growth).reshape(tok_rows, width_local * mode_count)
    lower_mask = (jnp.arange(tok_rows)[:, None] >= jnp.arange(tok_rows)[None, :]).astype(
        jnp.float32
    )
    running_sum = jnp.dot(lower_mask, scaled, precision=exact_mode).reshape(
        tok_rows, width_local, mode_count
    )
    shrink = jnp.exp(-decay_rate[None, :, :] * position[:, None, None])
    entering = (incoming * jnp.exp(-decay_rate))[None]
    convolved = jnp.sum(residue[None] * shrink * (running_sum + entering), axis=2)
    long_mix = convolved + skip_gain[None, :] * gated_wide
    return (query_gate * long_mix).astype(jnp.bfloat16)


def split_mesh(mesh):
    ctx, ch = (mesh.shape["ctx"], mesh.shape["ch"])
    inner = 4 if ctx % 4 == 0 else 1
    devices = np.asarray(mesh.devices).reshape(ctx // inner, inner, ch)
    return Mesh(devices, ("zl", "x", "ch"))


def solution(mesh):
    fine = split_mesh(mesh)
    in_specs = (
        P(SEQ, "ch"),
        P(SEQ, None, "ch"),
        P(None, None, "ch"),
        P("ch", None),
        P("ch", None),
        P("ch"),
    )
    out_specs = P(SEQ, "ch")
    return jax.shard_map(local, mesh=fine, in_specs=in_specs, out_specs=out_specs, check_vma=False)
```

profile of v0, /device:TPU:32, one launch (start us, length us, event | category | flops | bytes accessed | tf_op | source)
XLA Modules:
  0.0 327.1 jit_solution(8033702825253924592)
XLA Ops:
  7.3 82.0 %all-gather.2.cloned.1.call-done = bf16[256,8192]{1,0:T(8,128)(2,1)} async-done(((bf16[256,512]{1,0:T(8,128)(2,1)}), bf16[256,8192]{1,0:T(8,128)(2,1)}) %all-gather.2.cloned.1.call-update) | async-done | bytes 4194320 | tf_op jit(solution)/shard_map/all_gather | solution.py:35
  89.3 4.1 %constant_dynamic-slice_fusion.3 = (bf16[256,2048]{1,0:T(8,128)(2,1)S(1)}, bf16[256,2048]{1,0:T(8,128)(2,1)}, bf16[256,2048]{1,0:T(8,128)(2,1)}, bf16[256,2048]{1,0:T(8,128)(2,1)}) fusion(bf16[256,8192]{1,0:T(8,128)(2,1)} %all-gather.2.cloned.1.call-done, s32[]{:T(128)S(6)} %select_n.86, s32[]{:T(128)S(6)} %select_n.92, s32[]{:T(128)S(6)} %select_n.90, ...), kind=kLoop, calls=%fused_computation.55 | loop fusion | bytes 8388624 | tf_op jit(solution)/shard_map/dynamic_slice | solution.py:39
  93.7 2.9 collective-permute-start.1
  96.9 1.6 copy.17
  98.4 1.5 collective-permute-start.3
  99.9 2.7 collective-permute-start.4
  102.6 17.1 %collective-permute-done = bf16[256,2048]{1,0:T(8,128)(2,1)} collective-permute-done((bf16[256,2048]{1,0:T(8,128)(2,1)}, bf16[256,2048]{1,0:T(8,128)(2,1)}, u32[]{:S(2)}, u32[]{:S(2)}) %collective-permute-start) | collective-permute-done | bytes 1048608 | tf_op jit(solution)/shard_map/ppermute | solution.py:22
  119.7 2.7 collective-permute-start.5
  122.4 61.9 %collective-permute-done.1 = bf16[256,2048]{1,0:T(8,128)(2,1)} collective-permute-done((bf16[256,2048]{1,0:T(8,128)(2,1)}, bf16[256,2048]{1,0:T(8,128)(2,1)}, u32[]{:S(2)}, u32[]{:S(2)}) %collective-permute-start.1) | collective-permute-done | bytes 1048608 | tf_op jit(solution)/shard_map/ppermute | solution.py:22
  184.2 3.4 %collective-permute-done.2 = bf16[256,2048]{1,0:T(8,128)(2,1)} collective-permute-done((bf16[256,2048]{1,0:T(8,128)(2,1)}, bf16[256,2048]{1,0:T(8,128)(2,1)}, u32[]{:S(2)}, u32[]{:S(2)}) %collective-permute-start.2) | collective-permute-done | bytes 1048608 | tf_op jit(solution)/shard_map/ppermute | solution.py:22
  187.6 2.1 pad_maximum_fusion
  190.0 1.8 fusion.17
  191.8 5.9 %fusion.15 = f32[1024,1536]{1,0:T(8,128)} fusion(bf16[512,1536]{0,1:T(8,128)(2,1)} %collective-permute-done.3, bf16[1024,2048]{1,0:T(8,128)(2,1)S(1)} %pad_maximum_fusion, s32[]{:T(128)S(6)} %select_n.96), kind=kOutput, calls=%fused_computation.20 | convolution fusion | flops 1610612736 | bytes 8912900 | tf_op jit(solution)/shard_map/dot_general | solution.py:47
  197.7 4.4 %fusion.13 = f32[1024,1536]{1,0:T(8,128)} fusion(bf16[512,1536]{0,1:T(8,128)(2,1)S(1)} %collective-permute-done.4, bf16[1024,2048]{1,0:T(8,128)(2,1)S(1)} %pad_maximum_fusion, s32[]{:T(128)S(6)} %select_n.98), kind=kOutput, calls=%fused_computation.18 | convolution fusion | flops 1610612736 | bytes 8912900 | tf_op jit(solution)/shard_map/dot_general | solution.py:47
  202.1 7.4 %fusion.35 = (bf16[1024,1536]{1,0:T(8,128)(2,1)S(1)}, f32[1024,1536]{1,0:T(8,128)S(1)}) fusion(bf16[512,1536]{0,1:T(8,128)(2,1)} %collective-permute-done.5, bf16[1024,2048]{1,0:T(8,128)(2,1)S(1)} %pad_maximum_fusion, s32[]{:T(128)S(6)} %select_n.100, f32[1024,1536]{1,0:T(8,128)} %fusion.13, f32[1024,1536]{1,0:T(8,128)S(1)} %fusion.17, f32[1024,1536]{1,0:T(8,128)} %fusion.15), kind=kOutput, calls=%fused_computation.64 | convolution fusion | flops 1616904192 | bytes 30932996 | tf_op jit(solution)/shard_map/dot_general | solution.py:47
  210.0 1.0 collective-permute-start.7
  211.0 1.9 collective-permute-start.8
  212.9 51.2 %collective-permute-done.6 = bf16[256,1536]{1,0:T(8,128)(2,1)S(1)} collective-permute-done((bf16[256,1536]{1,0:T(8,128)(2,1)S(1)}, bf16[256,1536]{1,0:T(8,128)(2,1)S(1)}, u32[]{:S(2)}, u32[]{:S(2)}) %collective-permute-start.6) | collective-permute-done | bytes 786464 | tf_op jit(solution)/shard_map/ppermute | solution.py:52
  264.1 13.7 %collective-permute-done.8 = bf16[256,1536]{1,0:T(8,128)(2,1)S(1)} collective-permute-done((bf16[256,1536]{1,0:T(8,128)(2,1)S(1)}, bf16[256,1536]{1,0:T(8,128)(2,1)S(1)}, u32[]{:S(2)}, u32[]{:S(2)}) %collective-permute-start.8) | collective-permute-done | bytes 786464 | tf_op jit(solution)/shard_map/ppermute | solution.py:52
  278.2 3.4 %collective-permute-start.9 = (bf16[2,3,512]{2,0,1:T(2,128)(2,1)S(1)}, bf16[2,3,512]{2,0,1:T(2,128)(2,1)S(1)}, u32[]{:S(2)}, u32[]{:S(2)}) collective-permute-start(bf16[2,3,512]{2,0,1:T(2,128)(2,1)S(1)} %bitcast.57), channel_id=1, source_target_pairs={{0,16},{16,32},{32,48},{48,64},{64,80},{80,96},{96,112},{112,128},... | collective-permute-start | bytes 18440 | tf_op jit(solution)/shard_map/ppermute | solution.py:14
  282.2 5.2 %collective-permute-done.9 = bf16[2,3,512]{2,0,1:T(2,128)(2,1)S(1)} collective-permute-done((bf16[2,3,512]{2,0,1:T(2,128)(2,1)S(1)}, bf16[2,3,512]{2,0,1:T(2,128)(2,1)S(1)}, u32[]{:S(2)}, u32[]{:S(2)}) %collective-permute-start.9) | collective-permute-done | bytes 6176 | tf_op jit(solution)/shard_map/ppermute | solution.py:14
  288.3 1.5 multiply_reduce_fusion
  290.5 2.5 collective-permute-start.12
  293.4 1.5 collective-permute-done.10
  296.2 1.0 collective-permute-start.13
  297.2 3.0 collective-permute-start.14
  300.6 1.3 bitcast_multiply_fusion
  301.8 2.8 collective-permute-done.13
  304.6 1.4 collective-permute-done.14
  306.1 2.1 collective-permute-done.15
  308.2 1.1 fusion.22
  309.3 10.1 %multiply_reduce_fusion.1 = f32[256,512]{1,0:T(8,128)S(1)} fusion(f32[512,16]{0,1:T(8,128)S(1)} %exponential_multiply_fusion, f32[512,16]{0,1:T(8,128)S(1)} %neg.8, f32[512,16]{0,1:T(8,128)S(1)} %copy-done.5, f32[512,16,256]{2,1,0:T(8,128)S(1)} %bitcast.45), kind=kOutput, calls=%fused_computation.4 | convolution fusion | flops 6452871168 | bytes 9011200 | tf_op jit(solution)/shard_map/dot_general | solution.py:86
  (48 shorter events, 7.2 us)
Async XLA Ops:
  6.5 82.7 %all-gather.2.cloned.1.call-start = ((), (), s32[]{:S(2)}) async-start(), calls=%async_computation | async-start | bytes 4456448 | tf_op jit(solution)/shard_map/all_gather | solution.py:35
  7.3 89.5 %copy-start = (bf16[512,3,512]{2,0,1:T(8,128)(2,1)S(1)}, bf16[512,3,512]{2,0,1:T(8,128)(2,1)}, u32[]{:S(2)}) copy-start(bf16[512,3,512]{2,0,1:T(8,128)(2,1)} %param.7) | copy-start | bytes 4718596
  93.3 26.3 %collective-permute-start = (bf16[256,2048]{1,0:T(8,128)(2,1)}, bf16[256,2048]{1,0:T(8,128)(2,1)}, u32[]{:S(2)}, u32[]{:S(2)}) collective-permute-start(bf16[256,2048]{1,0:T(8,128)(2,1)} %get-tuple-element.10), channel_id=1, source_target_pairs={{0,64},{64,128},{128,192},{192,0},{1,65},{65,129},{129,193},{193,1... | collective-permute-start | bytes 3145736 | tf_op jit(solution)/shard_map/ppermute | solution.py:22
  93.7 90.6 %collective-permute-start.1 = (bf16[256,2048]{1,0:T(8,128)(2,1)}, bf16[256,2048]{1,0:T(8,128)(2,1)}, u32[]{:S(2)}, u32[]{:S(2)}) collective-permute-start(bf16[256,2048]{1,0:T(8,128)(2,1)} %get-tuple-element.9), channel_id=1, source_target_pairs={{0,128},{64,192},{128,0},{192,64},{1,129},{65,193},{129,1},{193,65... | collective-permute-start | bytes 3145736 | tf_op jit(solution)/shard_map/ppermute | solution.py:22
  96.6 91.0 %collective-permute-start.2 = (bf16[256,2048]{1,0:T(8,128)(2,1)}, bf16[256,2048]{1,0:T(8,128)(2,1)}, u32[]{:S(2)}, u32[]{:S(2)}) collective-permute-start(bf16[256,2048]{1,0:T(8,128)(2,1)} %get-tuple-element.8), channel_id=1, source_target_pairs={{0,192},{64,0},{128,64},{192,128},{1,193},{65,1},{129,65},{193,129... | collective-permute-start | bytes 3145736 | tf_op jit(solution)/shard_map/ppermute | solution.py:22
  98.4 93.3 %collective-permute-start.3 = (bf16[512,1536]{0,1:T(8,128)(2,1)}, bf16[512,1536]{0,1:T(8,128)(2,1)}, u32[]{:S(2)}, u32[]{:S(2)}) collective-permute-start(bf16[512,1536]{0,1:T(8,128)(2,1)} %bitcast.47), channel_id=1, source_target_pairs={{0,16},{16,32},{32,48},{48,0},{1,17},{17,33},{33,49},{49,1},{2,18}... | collective-permute-start | bytes 4718600 | tf_op jit(solution)/shard_map/ppermute | solution.py:22
  99.9 97.8 %collective-permute-start.4 = (bf16[512,1536]{0,1:T(8,128)(2,1)}, bf16[512,1536]{0,1:T(8,128)(2,1)S(1)}, u32[]{:S(2)}, u32[]{:S(2)}) collective-permute-start(bf16[512,1536]{0,1:T(8,128)(2,1)} %bitcast.48), channel_id=1, source_target_pairs={{0,32},{16,48},{32,0},{48,16},{1,33},{17,49},{33,1},{49,17},{2,34}... | collective-permute-start | bytes 4718600 | tf_op jit(solution)/shard_map/ppermute | solution.py:22
  119.7 82.5 %collective-permute-start.5 = (bf16[512,1536]{0,1:T(8,128)(2,1)}, bf16[512,1536]{0,1:T(8,128)(2,1)}, u32[]{:S(2)}, u32[]{:S(2)}) collective-permute-start(bf16[512,1536]{0,1:T(8,128)(2,1)} %bitcast.49), channel_id=1, source_target_pairs={{0,48},{16,0},{32,16},{48,32},{1,49},{17,1},{33,17},{49,33},{2,50}... | collective-permute-start | bytes 4718600 | tf_op jit(solution)/shard_map/ppermute | solution.py:22
  187.6 2.4 copy-start.1
  209.5 3.4 %copy-start.3 = (bf16[3,3,512]{2,1,0:T(4,128)(2,1)S(1)}, bf16[3,3,512]{2,1,0:T(4,128)(2,1)}, u32[]{:S(2)}) copy-start(bf16[3,3,512]{2,1,0:T(4,128)(2,1)} %param.8) | copy-start | bytes 27652
  209.5 72.1 %copy-start.2 = (f32[512,16]{0,1:T(8,128)S(1)}, f32[512,16]{0,1:T(8,128)}, u32[]{:S(2)}) copy-start(f32[512,16]{0,1:T(8,128)} %param.9) | copy-start | bytes 98308
  209.7 54.4 %collective-permute-start.6 = (bf16[256,1536]{1,0:T(8,128)(2,1)S(1)}, bf16[256,1536]{1,0:T(8,128)(2,1)S(1)}, u32[]{:S(2)}, u32[]{:S(2)}) collective-permute-start(bf16[256,1536]{1,0:T(8,128)(2,1)S(1)} %get-tuple-element.11), channel_id=1, source_target_pairs={{0,192},{64,0},{128,64},{192,128},{1,193},{65,1},{129,65},{193,129... | collective-permute-start | bytes 2359304 | tf_op jit(solution)/shard_map/ppermute | solution.py:52
  210.0 54.1 %collective-permute-start.7 = (bf16[256,1536]{1,0:T(8,128)(2,1)S(1)}, bf16[256,1536]{1,0:T(8,128)(2,1)S(1)}, u32[]{:S(2)}, u32[]{:S(2)}) collective-permute-start(bf16[256,1536]{1,0:T(8,128)(2,1)S(1)} %get-tuple-element.13), channel_id=1, source_target_pairs={{0,128},{64,192},{128,0},{192,64},{1,129},{65,193},{129,1},{193,65... | collective-permute-start | bytes 2359304 | tf_op jit(solution)/shard_map/ppermute | solution.py:52
  211.0 66.9 %collective-permute-start.8 = (bf16[256,1536]{1,0:T(8,128)(2,1)S(1)}, bf16[256,1536]{1,0:T(8,128)(2,1)S(1)}, u32[]{:S(2)}, u32[]{:S(2)}) collective-permute-start(bf16[256,1536]{1,0:T(8,128)(2,1)S(1)} %get-tuple-element.12), channel_id=1, source_target_pairs={{0,64},{64,128},{128,192},{192,0},{1,65},{65,129},{129,193},{193,1... | collective-permute-start | bytes 2359304 | tf_op jit(solution)/shard_map/ppermute | solution.py:52
  278.2 9.2 %collective-permute-start.9 = (bf16[2,3,512]{2,0,1:T(2,128)(2,1)S(1)}, bf16[2,3,512]{2,0,1:T(2,128)(2,1)S(1)}, u32[]{:S(2)}, u32[]{:S(2)}) collective-permute-start(bf16[2,3,512]{2,0,1:T(2,128)(2,1)S(1)} %bitcast.57), channel_id=1, source_target_pairs={{0,16},{16,32},{32,48},{48,64},{64,80},{80,96},{96,112},{112,128},... | collective-permute-start | bytes 18440 | tf_op jit(solution)/shard_map/ppermute | solution.py:14
  289.8 5.2 %collective-permute-start.10 = (f32[512,16]{0,1:T(8,128)S(1)}, f32[512,16]{0,1:T(8,128)S(1)}, u32[]{:S(2)}, u32[]{:S(2)}) collective-permute-start(f32[512,16]{0,1:T(8,128)S(1)} %multiply_reduce_fusion), channel_id=1, source_target_pairs={{0,16},{16,32},{32,48},{48,0},{1,17},{17,33},{33,49},{49,1},{2,18}... | collective-permute-start | bytes 98312 | tf_op jit(solution)/shard_map/ppermute | solution.py:22
  289.9 5.5 %collective-permute-start.11 = (f32[512,16]{0,1:T(8,128)S(1)}, f32[512,16]{0,1:T(8,128)S(1)}, u32[]{:S(2)}, u32[]{:S(2)}) collective-permute-start(f32[512,16]{0,1:T(8,128)S(1)} %multiply_reduce_fusion), channel_id=1, source_target_pairs={{0,32},{16,48},{32,0},{48,16},{1,33},{17,49},{33,1},{49,17},{2,34}... | collective-permute-start | bytes 98312 | tf_op jit(solution)/shard_map/ppermute | solution.py:22
  290.5 5.6 %collective-permute-start.12 = (f32[512,16]{0,1:T(8,128)S(1)}, f32[512,16]{0,1:T(8,128)S(1)}, u32[]{:S(2)}, u32[]{:S(2)}) collective-permute-start(f32[512,16]{0,1:T(8,128)S(1)} %multiply_reduce_fusion), channel_id=1, source_target_pairs={{0,48},{16,0},{32,16},{48,32},{1,49},{17,1},{33,17},{49,33},{2,50}... | collective-permute-start | bytes 98312 | tf_op jit(solution)/shard_map/ppermute | solution.py:22
  296.2 8.4 %collective-permute-start.13 = (f32[4,512,16]{1,2,0:T(8,128)S(1)}, f32[4,512,16]{1,2,0:T(8,128)S(1)}, u32[]{:S(2)}, u32[]{:S(2)}) collective-permute-start(f32[4,512,16]{1,2,0:T(8,128)S(1)} %get-tuple-element.15), channel_id=1, source_target_pairs={{0,64},{64,128},{128,192},{192,0},{1,65},{65,129},{129,193},{193,1... | collective-permute-start | bytes 393224 | tf_op jit(solution)/shard_map/ppermute | solution.py:22
  297.2 8.8 %collective-permute-start.14 = (f32[4,512,16]{1,2,0:T(8,128)S(1)}, f32[4,512,16]{1,2,0:T(8,128)S(1)}, u32[]{:S(2)}, u32[]{:S(2)}) collective-permute-start(f32[4,512,16]{1,2,0:T(8,128)S(1)} %get-tuple-element.15), channel_id=1, source_target_pairs={{0,128},{64,192},{128,0},{192,64},{1,129},{65,193},{129,1},{193,65... | collective-permute-start | bytes 393224 | tf_op jit(solution)/shard_map/ppermute | solution.py:22
  300.3 7.9 %collective-permute-start.15 = (f32[4,512,16]{1,2,0:T(8,128)S(1)}, f32[4,512,16]{1,2,0:T(8,128)}, u32[]{:S(2)}, u32[]{:S(2)}) collective-permute-start(f32[4,512,16]{1,2,0:T(8,128)S(1)} %get-tuple-element.15), channel_id=1, source_target_pairs={{0,192},{64,0},{128,64},{192,128},{1,193},{65,1},{129,65},{193,129... | collective-permute-start | bytes 393224 | tf_op jit(solution)/shard_map/ppermute | solution.py:22
  300.5 8.7 %copy-start.5 = (f32[512,16]{0,1:T(8,128)S(1)}, f32[512,16]{0,1:T(8,128)}, u32[]{:S(2)}) copy-start(f32[512,16]{0,1:T(8,128)} %param.10) | copy-start | bytes 98308
  309.3 10.1 %copy-start.4 = (f32[512]{0:T(512)S(1)}, f32[512]{0:T(512)}, u32[]{:S(2)}) copy-start(f32[512]{0:T(512)} %param.11) | copy-start | bytes 6148
Sparse Core Ops, SparseCore 0:
  9.9 79.3 all-gather.1
where the time goes:
time: 327 us
  waiting for transfers between devices  244 us (75%)
  matrix products  29.6 us (9%)
  starting transfers between devices  24.3 us (7%)
  between operations  13.7 us (4%)
  other arithmetic  8.26 us (3%)
  local copies, waits for them, and re-layouts  7.05 us (2%)
    ppermute x12, waiting for transfers between devices, ring_sends(): received.append(lax.ppermute(pieces(k, position), axis, route))  91.4 us
    all_gather x1, waiting for transfers between devices, local(): gathered = lax.all_gather(tokens, 'ch', axis=1, tiled=True)  82 us
    ppermute x3, waiting for transfers between devices, local(): back = lax.ppermute(pieces[k].astype(jnp.bfloat16), 'zl', route)  64.9 us
    dot_general x4, matrix products, local(): jnp.dot(taken, weights[k], preferred_element_type=jnp.float32)  19.5 us
    ppermute x12, starting transfers between devices, ring_sends(): received.append(lax.ppermute(pieces(k, position), axis, route))  17.7 us
    dot_general x1, matrix products, local(): jnp.dot(lower_mask, scaled, precision=exact_mode)  10.1 us
  transfers between devices with their start and end apart: 17, of which 13 were waited for; matrix products, arithmetic and copies ran while one was open for 6% of the time, Pallas kernels for 0%

commit v1 on v0

--- a/solution.py
+++ b/solution.py
@@ -32,7 +32,9 @@
     me_x, me_z = (lax.axis_index("x"), lax.axis_index("zl"))
     flat_own = in_weight.reshape(feat_block, 3 * width_local)
     weights = [flat_own] + ring_sends(lambda k, p: flat_own, "x", across)
-    gathered = lax.all_gather(tokens, "ch", axis=1, tiled=True)
+    gathered = jnp.concatenate(
+        lax.all_to_all(jnp.stack([tokens] * lax.axis_size("ch")), "ch", 0, 0), axis=1
+    )
     chunk = gathered.shape[1] // down
 
     def chunk_for(k, p):

time: 327 us -> 340 us (1.040)
  between operations: 13.7 us -> 0.35 us
  starting transfers between devices: 24.3 us -> 37.6 us
  waiting for transfers between devices: 244 us -> 254 us
  local copies, waits for them, and re-layouts: 7.05 us -> 10.5 us
    all_to_all x0 -> x1, waiting for transfers between devices: none -> 99.2 us  [local(): lax.all_to_all(jnp.stack([tokens] * lax.axis_size('ch')), 'ch', 0, 0)]
    all_gather x1 -> x0, waiting for transfers between devices: 82 us -> none  [local(): gathered = lax.all_gather(tokens, 'ch', axis=1, tiled=True)]
    all_to_all x0 -> x1, starting transfers between devices: none -> 10.4 us  [local(): lax.all_to_all(jnp.stack([tokens] * lax.axis_size('ch')), 'ch', 0, 0)]
    ppermute x12, waiting for transfers between devices: 91.4 us -> 87.7 us  [ring_sends(): received.append(lax.ppermute(pieces(k, position), axis, route))]
  transfers between devices with their start and end apart: 17 -> 17, of which waited for: 13 -> 12; matrix products, arithmetic and copies ran while one was open for 6% -> 5% of each run, Pallas kernels for 0% -> 0%
where the time goes in v1:
time: 340 us
  waiting for transfers between devices  254 us (75%)
  starting transfers between devices  37.6 us (11%)
  matrix products  29.6 us (9%)
  local copies, waits for them, and re-layouts  10.5 us (3%)
  other arithmetic  8.38 us (2%)
    all_to_all x1, waiting for transfers between devices, local(): lax.all_to_all(jnp.stack([tokens] * lax.axis_size('ch')), 'ch', 0, 0)  99.2 us
    ppermute x12, waiting for transfers between devices, ring_sends(): received.append(lax.ppermute(pieces(k, position), axis, route))  87.7 us
    ppermute x3, waiting for transfers between devices, local(): back = lax.ppermute(pieces[k].astype(jnp.bfloat16), 'zl', route)  63.3 us
    dot_general x4, matrix products, local(): jnp.dot(taken, weights[k], preferred_element_type=jnp.float32)  19.6 us
    ppermute x12, starting transfers between devices, ring_sends(): received.append(lax.ppermute(pieces(k, position), axis, route))  17.3 us
    all_to_all x1, starting transfers between devices, local(): lax.all_to_all(jnp.stack([tokens] * lax.axis_size('ch')), 'ch', 0, 0)  10.4 us
    dot_general x1, matrix products, local(): jnp.dot(lower_mask, scaled, precision=exact_mode)  10.1 us
  transfers between devices with their start and end apart: 17, of which 12 were waited for; matrix products, arithmetic and copies ran while one was open for 5% of the time, Pallas kernels for 0%

profile of v1, /device:TPU:32, one launch (start us, length us, event | category | flops | bytes accessed | tf_op | source)
XLA Modules:
  0.0 340.1 jit_solution(8998982436846588221)
XLA Ops:
  1.1 2.4 stack.22
  3.5 10.4 %all-to-all-start = ((bf16[16,256,512]{1,2,0:T(8,128)(2,1)}), bf16[16,256,512]{1,2,0:T(8,128)(2,1)}, u32[]{:S(2)}, u32[]{:S(2)}) async-start(bf16[16,256,512]{1,2,0:T(8,128)(2,1)} %stack.22), calls=%async_computation | async-start | bytes 8388608 | tf_op jit(solution)/shard_map/all_to_all | solution.py:36
  13.9 99.2 %all-to-all-done = bf16[16,256,512]{1,2,0:T(8,128)(2,1)} async-done(((bf16[16,256,512]{1,2,0:T(8,128)(2,1)}), bf16[16,256,512]{1,2,0:T(8,128)(2,1)}, u32[]{:S(2)}, u32[]{:S(2)}) %all-to-all-start) | async-done | bytes 4194336 | tf_op jit(solution)/shard_map/all_to_all | solution.py:36
  113.1 4.1 %constant_dynamic-slice_fusion.3 = (bf16[256,2048]{0,1:T(8,128)(2,1)S(1)}, bf16[256,2048]{0,1:T(8,128)(2,1)}, bf16[256,2048]{0,1:T(8,128)(2,1)}, bf16[256,2048]{0,1:T(8,128)(2,1)}) fusion(bf16[256,8192]{0,1:T(8,128)(2,1)} %bitcast.4, s32[]{:T(128)S(6)} %select_n.86, s32[]{:T(128)S(6)} %select_n.92, s32[]{:T(128)S(6)} %select_n.90, s32[]{:T(128)S(6)} %select_n.88), kind=kLoop, calls=%fused_computation.55 | loop fusion | bytes 8388624 | tf_op jit(solution)/shard_map/dynamic_slice | solution.py:41
  118.3 1.5 collective-permute-start.2
  119.8 1.6 copy.19
  121.4 1.5 collective-permute-start.3
  122.9 2.7 collective-permute-start.4
  125.6 61.5 %collective-permute-done = bf16[256,2048]{0,1:T(8,128)(2,1)} collective-permute-done((bf16[256,2048]{0,1:T(8,128)(2,1)}, bf16[256,2048]{0,1:T(8,128)(2,1)}, u32[]{:S(2)}, u32[]{:S(2)}) %collective-permute-start) | collective-permute-done | bytes 1048608 | tf_op jit(solution)/shard_map/ppermute | solution.py:22
  187.1 2.8 collective-permute-start.5
  189.9 18.2 %collective-permute-done.1 = bf16[256,2048]{0,1:T(8,128)(2,1)} collective-permute-done((bf16[256,2048]{0,1:T(8,128)(2,1)}, bf16[256,2048]{0,1:T(8,128)(2,1)}, u32[]{:S(2)}, u32[]{:S(2)}) %collective-permute-start.1) | collective-permute-done | bytes 1048608 | tf_op jit(solution)/shard_map/ppermute | solution.py:22
  208.1 2.3 pad_maximum_fusion
  210.5 1.8 fusion.17
  212.3 5.9 %fusion.15 = f32[1024,1536]{1,0:T(8,128)} fusion(bf16[512,1536]{0,1:T(8,128)(2,1)} %collective-permute-done.3, bf16[1024,2048]{0,1:T(8,128)(2,1)S(1)} %pad_maximum_fusion, s32[]{:T(128)S(6)} %select_n.96), kind=kOutput, calls=%fused_computation.20 | convolution fusion | flops 1610612736 | bytes 8912900 | tf_op jit(solution)/shard_map/dot_general | solution.py:49
  218.2 4.5 %fusion.13 = f32[1024,1536]{1,0:T(8,128)} fusion(bf16[512,1536]{0,1:T(8,128)(2,1)S(1)} %collective-permute-done.4, bf16[1024,2048]{0,1:T(8,128)(2,1)S(1)} %pad_maximum_fusion, s32[]{:T(128)S(6)} %select_n.98), kind=kOutput, calls=%fused_computation.18 | convolution fusion | flops 1610612736 | bytes 8912900 | tf_op jit(solution)/shard_map/dot_general | solution.py:49
  222.7 7.3 %fusion.35 = (bf16[1024,1536]{1,0:T(8,128)(2,1)S(1)}, f32[1024,1536]{1,0:T(8,128)S(1)}) fusion(bf16[512,1536]{0,1:T(8,128)(2,1)} %collective-permute-done.5, bf16[1024,2048]{0,1:T(8,128)(2,1)S(1)} %pad_maximum_fusion, s32[]{:T(128)S(6)} %select_n.100, f32[1024,1536]{1,0:T(8,128)} %fusion.13, f32[1024,1536]{1,0:T(8,128)S(1)} %fusion.17, f32[1024,1536]{1,0:T(8,128)} %fusion.15), kind=kOutput, calls=%fused_computation.64 | convolution fusion | flops 1616904192 | bytes 30932996 | tf_op jit(solution)/shard_map/dot_general | solution.py:49
  230.3 3.5 %collective-permute-start.7 = (bf16[256,1536]{1,0:T(8,128)(2,1)S(1)}, bf16[256,1536]{1,0:T(8,128)(2,1)S(1)}, u32[]{:S(2)}, u32[]{:S(2)}) collective-permute-start(bf16[256,1536]{1,0:T(8,128)(2,1)S(1)} %get-tuple-element.13), channel_id=1, source_target_pairs={{0,128},{64,192},{128,0},{192,64},{1,129},{65,193},{129,1},{193,65... | collective-permute-start | bytes 2359304 | tf_op jit(solution)/shard_map/ppermute | solution.py:54
  233.8 2.8 collective-permute-start.8
  236.7 47.8 %collective-permute-done.6 = bf16[256,1536]{1,0:T(8,128)(2,1)S(1)} collective-permute-done((bf16[256,1536]{1,0:T(8,128)(2,1)S(1)}, bf16[256,1536]{1,0:T(8,128)(2,1)S(1)}, u32[]{:S(2)}, u32[]{:S(2)}) %collective-permute-start.6) | collective-permute-done | bytes 786464 | tf_op jit(solution)/shard_map/ppermute | solution.py:54
  284.4 15.6 %collective-permute-done.8 = bf16[256,1536]{1,0:T(8,128)(2,1)S(1)} collective-permute-done((bf16[256,1536]{1,0:T(8,128)(2,1)S(1)}, bf16[256,1536]{1,0:T(8,128)(2,1)S(1)}, u32[]{:S(2)}, u32[]{:S(2)}) %collective-permute-start.8) | collective-permute-done | bytes 786464 | tf_op jit(solution)/shard_map/ppermute | solution.py:54
  300.4 3.6 %collective-permute-start.9 = (bf16[2,3,512]{2,0,1:T(2,128)(2,1)S(1)}, bf16[2,3,512]{2,0,1:T(2,128)(2,1)S(1)}, u32[]{:S(2)}, u32[]{:S(2)}) collective-permute-start(bf16[2,3,512]{2,0,1:T(2,128)(2,1)S(1)} %bitcast.60), channel_id=1, source_target_pairs={{0,16},{16,32},{32,48},{48,64},{64,80},{80,96},{96,112},{112,128},... | collective-permute-start | bytes 18440 | tf_op jit(solution)/shard_map/ppermute | solution.py:14
  304.6 3.4 %collective-permute-done.9 = bf16[2,3,512]{2,0,1:T(2,128)(2,1)S(1)} collective-permute-done((bf16[2,3,512]{2,0,1:T(2,128)(2,1)S(1)}, bf16[2,3,512]{2,0,1:T(2,128)(2,1)S(1)}, u32[]{:S(2)}, u32[]{:S(2)}) %collective-permute-start.9) | collective-permute-done | bytes 6176 | tf_op jit(solution)/shard_map/ppermute | solution.py:14
  308.9 1.5 multiply_reduce_fusion
  310.5 2.2 collective-permute-start.11
  312.7 1.3 collective-permute-start.12
  314.4 1.2 collective-permute-done.10
  316.8 2.6 collective-permute-start.13
  319.4 1.6 collective-permute-start.15
  321.3 1.3 bitcast_multiply_fusion
  322.5 2.1 collective-permute-done.13
  324.6 2.8 collective-permute-done.14
  329.2 10.1 %multiply_reduce_fusion.1 = f32[256,512]{1,0:T(8,128)S(1)} fusion(f32[512,16]{0,1:T(8,128)S(1)} %exponential_multiply_fusion, f32[512,16]{0,1:T(8,128)S(1)} %neg.8, f32[512,16]{0,1:T(8,128)S(1)} %copy-done.5, f32[512,16,256]{2,1,0:T(8,128)S(1)} %bitcast.48), kind=kOutput, calls=%fused_computation.4 | convolution fusion | flops 6452871168 | bytes 9011200 | tf_op jit(solution)/shard_map/dot_general | solution.py:88
  (49 shorter events, 8.9 us)
Async XLA Ops:
  3.5 109.6 %all-to-all-start = ((bf16[16,256,512]{1,2,0:T(8,128)(2,1)}), bf16[16,256,512]{1,2,0:T(8,128)(2,1)}, u32[]{:S(2)}, u32[]{:S(2)}) async-start(bf16[16,256,512]{1,2,0:T(8,128)(2,1)} %stack.22), calls=%async_computation | async-start | bytes 8388608 | tf_op jit(solution)/shard_map/all_to_all | solution.py:36
  113.1 6.6 %copy-start = (bf16[512,3,512]{2,0,1:T(8,128)(2,1)S(1)}, bf16[512,3,512]{2,0,1:T(8,128)(2,1)}, u32[]{:S(2)}) copy-start(bf16[512,3,512]{2,0,1:T(8,128)(2,1)} %param.7) | copy-start | bytes 4718596
  117.2 69.9 %collective-permute-start = (bf16[256,2048]{0,1:T(8,128)(2,1)}, bf16[256,2048]{0,1:T(8,128)(2,1)}, u32[]{:S(2)}, u32[]{:S(2)}) collective-permute-start(bf16[256,2048]{0,1:T(8,128)(2,1)} %get-tuple-element.10), channel_id=1, source_target_pairs={{0,64},{64,128},{128,192},{192,0},{1,65},{65,129},{129,193},{193,1... | collective-permute-start | bytes 3145736 | tf_op jit(solution)/shard_map/ppermute | solution.py:22
  118.3 89.8 %collective-permute-start.1 = (bf16[256,2048]{0,1:T(8,128)(2,1)}, bf16[256,2048]{0,1:T(8,128)(2,1)}, u32[]{:S(2)}, u32[]{:S(2)}) collective-permute-start(bf16[256,2048]{0,1:T(8,128)(2,1)} %get-tuple-element.9), channel_id=1, source_target_pairs={{0,128},{64,192},{128,0},{192,64},{1,129},{65,193},{129,1},{193,65... | collective-permute-start | bytes 3145736 | tf_op jit(solution)/shard_map/ppermute | solution.py:22
  118.3 89.8 %collective-permute-start.2 = (bf16[256,2048]{0,1:T(8,128)(2,1)}, bf16[256,2048]{0,1:T(8,128)(2,1)}, u32[]{:S(2)}, u32[]{:S(2)}) collective-permute-start(bf16[256,2048]{0,1:T(8,128)(2,1)} %get-tuple-element.8), channel_id=1, source_target_pairs={{0,192},{64,0},{128,64},{192,128},{1,193},{65,1},{129,65},{193,129... | collective-permute-start | bytes 3145736 | tf_op jit(solution)/shard_map/ppermute | solution.py:22
  121.4 90.9 %collective-permute-start.3 = (bf16[512,1536]{0,1:T(8,128)(2,1)}, bf16[512,1536]{0,1:T(8,128)(2,1)}, u32[]{:S(2)}, u32[]{:S(2)}) collective-permute-start(bf16[512,1536]{0,1:T(8,128)(2,1)} %bitcast.50), channel_id=1, source_target_pairs={{0,16},{16,32},{32,48},{48,0},{1,17},{17,33},{33,49},{49,1},{2,18}... | collective-permute-start | bytes 4718600 | tf_op jit(solution)/shard_map/ppermute | solution.py:22
  122.9 95.4 %collective-permute-start.4 = (bf16[512,1536]{0,1:T(8,128)(2,1)}, bf16[512,1536]{0,1:T(8,128)(2,1)S(1)}, u32[]{:S(2)}, u32[]{:S(2)}) collective-permute-start(bf16[512,1536]{0,1:T(8,128)(2,1)} %bitcast.51), channel_id=1, source_target_pairs={{0,32},{16,48},{32,0},{48,16},{1,33},{17,49},{33,1},{49,17},{2,34}... | collective-permute-start | bytes 4718600 | tf_op jit(solution)/shard_map/ppermute | solution.py:22
  187.1 35.6 %collective-permute-start.5 = (bf16[512,1536]{0,1:T(8,128)(2,1)}, bf16[512,1536]{0,1:T(8,128)(2,1)}, u32[]{:S(2)}, u32[]{:S(2)}) collective-permute-start(bf16[512,1536]{0,1:T(8,128)(2,1)} %bitcast.52), channel_id=1, source_target_pairs={{0,48},{16,0},{32,16},{48,32},{1,49},{17,1},{33,17},{49,33},{2,50}... | collective-permute-start | bytes 4718600 | tf_op jit(solution)/shard_map/ppermute | solution.py:22
  208.1 2.4 copy-start.1
  230.1 6.6 %copy-start.3 = (bf16[3,3,512]{2,1,0:T(4,128)(2,1)S(1)}, bf16[3,3,512]{2,1,0:T(4,128)(2,1)}, u32[]{:S(2)}) copy-start(bf16[3,3,512]{2,1,0:T(4,128)(2,1)} %param.8) | copy-start | bytes 27652
  230.1 74.0 %copy-start.2 = (f32[512,16]{0,1:T(8,128)S(1)}, f32[512,16]{0,1:T(8,128)}, u32[]{:S(2)}) copy-start(f32[512,16]{0,1:T(8,128)} %param.9) | copy-start | bytes 98308
  230.2 54.2 %collective-permute-start.6 = (bf16[256,1536]{1,0:T(8,128)(2,1)S(1)}, bf16[256,1536]{1,0:T(8,128)(2,1)S(1)}, u32[]{:S(2)}, u32[]{:S(2)}) collective-permute-start(bf16[256,1536]{1,0:T(8,128)(2,1)S(1)} %get-tuple-element.11), channel_id=1, source_target_pairs={{0,192},{64,0},{128,64},{192,128},{1,193},{65,1},{129,65},{193,129... | collective-permute-start | bytes 2359304 | tf_op jit(solution)/shard_map/ppermute | solution.py:54
  230.3 54.1 %collective-permute-start.7 = (bf16[256,1536]{1,0:T(8,128)(2,1)S(1)}, bf16[256,1536]{1,0:T(8,128)(2,1)S(1)}, u32[]{:S(2)}, u32[]{:S(2)}) collective-permute-start(bf16[256,1536]{1,0:T(8,128)(2,1)S(1)} %get-tuple-element.13), channel_id=1, source_target_pairs={{0,128},{64,192},{128,0},{192,64},{1,129},{65,193},{129,1},{193,65... | collective-permute-start | bytes 2359304 | tf_op jit(solution)/shard_map/ppermute | solution.py:54
  233.8 66.2 %collective-permute-start.8 = (bf16[256,1536]{1,0:T(8,128)(2,1)S(1)}, bf16[256,1536]{1,0:T(8,128)(2,1)S(1)}, u32[]{:S(2)}, u32[]{:S(2)}) collective-permute-start(bf16[256,1536]{1,0:T(8,128)(2,1)S(1)} %get-tuple-element.12), channel_id=1, source_target_pairs={{0,64},{64,128},{128,192},{192,0},{1,65},{65,129},{129,193},{193,1... | collective-permute-start | bytes 2359304 | tf_op jit(solution)/shard_map/ppermute | solution.py:54
  300.4 7.6 %collective-permute-start.9 = (bf16[2,3,512]{2,0,1:T(2,128)(2,1)S(1)}, bf16[2,3,512]{2,0,1:T(2,128)(2,1)S(1)}, u32[]{:S(2)}, u32[]{:S(2)}) collective-permute-start(bf16[2,3,512]{2,0,1:T(2,128)(2,1)S(1)} %bitcast.60), channel_id=1, source_target_pairs={{0,16},{16,32},{32,48},{48,64},{64,80},{80,96},{96,112},{112,128},... | collective-permute-start | bytes 18440 | tf_op jit(solution)/shard_map/ppermute | solution.py:14
  310.4 5.2 %collective-permute-start.10 = (f32[512,16]{0,1:T(8,128)S(1)}, f32[512,16]{0,1:T(8,128)S(1)}, u32[]{:S(2)}, u32[]{:S(2)}) collective-permute-start(f32[512,16]{0,1:T(8,128)S(1)} %multiply_reduce_fusion), channel_id=1, source_target_pairs={{0,16},{16,32},{32,48},{48,0},{1,17},{17,33},{33,49},{49,1},{2,18}... | collective-permute-start | bytes 98312 | tf_op jit(solution)/shard_map/ppermute | solution.py:22
  310.5 5.5 %collective-permute-start.11 = (f32[512,16]{0,1:T(8,128)S(1)}, f32[512,16]{0,1:T(8,128)S(1)}, u32[]{:S(2)}, u32[]{:S(2)}) collective-permute-start(f32[512,16]{0,1:T(8,128)S(1)} %multiply_reduce_fusion), channel_id=1, source_target_pairs={{0,32},{16,48},{32,0},{48,16},{1,33},{17,49},{33,1},{49,17},{2,34}... | collective-permute-start | bytes 98312 | tf_op jit(solution)/shard_map/ppermute | solution.py:22
  312.7 4.1 %collective-permute-start.12 = (f32[512,16]{0,1:T(8,128)S(1)}, f32[512,16]{0,1:T(8,128)S(1)}, u32[]{:S(2)}, u32[]{:S(2)}) collective-permute-start(f32[512,16]{0,1:T(8,128)S(1)} %multiply_reduce_fusion), channel_id=1, source_target_pairs={{0,48},{16,0},{32,16},{48,32},{1,49},{17,1},{33,17},{49,33},{2,50}... | collective-permute-start | bytes 98312 | tf_op jit(solution)/shard_map/ppermute | solution.py:22
  316.8 7.8 %collective-permute-start.13 = (f32[4,512,16]{1,2,0:T(8,128)S(1)}, f32[4,512,16]{1,2,0:T(8,128)S(1)}, u32[]{:S(2)}, u32[]{:S(2)}) collective-permute-start(f32[4,512,16]{1,2,0:T(8,128)S(1)} %get-tuple-element.15), channel_id=1, source_target_pairs={{0,64},{64,128},{128,192},{192,0},{1,65},{65,129},{129,193},{193,1... | collective-permute-start | bytes 393224 | tf_op jit(solution)/shard_map/ppermute | solution.py:22
  319.4 8.0 %collective-permute-start.14 = (f32[4,512,16]{1,2,0:T(8,128)S(1)}, f32[4,512,16]{1,2,0:T(8,128)S(1)}, u32[]{:S(2)}, u32[]{:S(2)}) collective-permute-start(f32[4,512,16]{1,2,0:T(8,128)S(1)} %get-tuple-element.15), channel_id=1, source_target_pairs={{0,128},{64,192},{128,0},{192,64},{1,129},{65,193},{129,1},{193,65... | collective-permute-start | bytes 393224 | tf_op jit(solution)/shard_map/ppermute | solution.py:22
  319.4 8.6 %collective-permute-start.15 = (f32[4,512,16]{1,2,0:T(8,128)S(1)}, f32[4,512,16]{1,2,0:T(8,128)}, u32[]{:S(2)}, u32[]{:S(2)}) collective-permute-start(f32[4,512,16]{1,2,0:T(8,128)S(1)} %get-tuple-element.15), channel_id=1, source_target_pairs={{0,192},{64,0},{128,64},{192,128},{1,193},{65,1},{129,65},{193,129... | collective-permute-start | bytes 393224 | tf_op jit(solution)/shard_map/ppermute | solution.py:22
  321.2 7.9 %copy-start.5 = (f32[512,16]{0,1:T(8,128)S(1)}, f32[512,16]{0,1:T(8,128)}, u32[]{:S(2)}) copy-start(f32[512,16]{0,1:T(8,128)} %param.10) | copy-start | bytes 98308
  329.2 10.1 %copy-start.4 = (f32[512]{0:T(512)S(1)}, f32[512]{0:T(512)}, u32[]{:S(2)}) copy-start(f32[512]{0:T(512)} %param.11) | copy-start | bytes 6148
